TPU v7x, 128 devices: a whole 4x4x4 slice. The times are simulated.
128 devices in a mesh: seq: 32 (over y, z, core), head: 4 (over x).
Axes of the slice: x: 4, y: 4, z: 4, core: 2. Of those that a mesh axis runs over, the one named last changes fastest.
Arguments:
- queries: bfloat16 [8192, 2048], P('seq', 'head'), parts along dimension 1, may hold values from -6 to 6
- keys: bfloat16 [8192, 512], P('seq', 'head'), parts along dimension 1, may hold values from -6 to 6
- values: bfloat16 [8192, 512], P('seq', 'head'), parts along dimension 1, may hold values from -6 to 6
- grad_out: bfloat16 [8192, 2048], P('seq', 'head'), parts along dimension 1, may hold values from -6 to 6
- lengths: int32 [16], replicated, may hold values from 1 to 2048, 8192 in all
- send_order: int32 [32, 256], replicated, may hold values from 0 to 255, each once within a row
Outputs:
- attended: float32 [8192, 2048], P('seq', 'head'), parts along dimension 1
- grad_queries: float32 [8192, 2048], P('seq', 'head'), parts along dimension 1
- grad_keys: float32 [8192, 512], P('seq', 'head'), parts along dimension 1
- grad_values: float32 [8192, 512], P('seq', 'head'), parts along dimension 1
There are 4 independent parts, one for each index of `head`. A program takes and returns all parts, laid end to end along the dimension named above; an argument that names none is the same for every part. Nothing has to cross between parts.
Inputs may be any that keep to these rules, and one draw needn't show every extreme that they name: `lengths`: they sum to 8192; the longest is exactly 2048. `send_order`: each row is a permutation of 0 to 255.
All inputs are finite; a program needn't handle non-finite values.
Results may differ from a plain program's by a relative error of at most 0.039.
Values may be sent and summed in bfloat16 or wider, within the bound.
No kernel may reach another device: no remote copies, remote signals or barrier semaphores. Data moves between devices by JAX's collectives and lax.ppermute only.
A program may use at most 64 MiB of HBM per device.

v0:
```python
import math
import jax
import jax.numpy as jnp
from jax import lax
from jax.sharding import PartitionSpec as P

masked_value = -1e30


def doc_index(positions, bounds):
    return jnp.sum((positions[:, None] >= bounds[None, :]).astype(jnp.int32), axis=1)


def visible(query_pos, query_doc, key_pos, bounds):
    key_doc = doc_index(key_pos, bounds)
    return ((query_doc[:, None] == key_doc[None, :]) & (key_pos[None, :] <= query_pos[:, None]))[
        :, None, :
    ]


def block_scores(query_heads, key_block, allowed, score_scale):
    products = (
        jnp.einsum("bhd,td->bht", query_heads, key_block, preferred_element_type=jnp.float32)
        * score_scale
    )
    return jnp.where(allowed, products, masked_value)


def key_blocks(key_piece, value_piece):
    piece_rows = key_piece.shape[0]
    block_rows = math.gcd(piece_rows, 512)
    block_count = piece_rows // block_rows
    offsets = block_rows * jnp.arange(block_count, dtype=jnp.int32)
    stacked = (
        key_piece.reshape(block_count, block_rows, key_piece.shape[1]),
        value_piece.reshape(block_count, block_rows, value_piece.shape[1]),
        offsets,
    )
    return (stacked, block_rows)


def forward_piece(run_state, key_piece, value_piece, context):
    query_heads, query_pos, query_doc, bounds, score_scale = context
    stacked, block_rows = key_blocks(key_piece, value_piece)

    def forward_update(loop_state, block_item):
        run_max, run_total, weighted = loop_state
        key_block, value_block, offset = block_item
        allowed = visible(
            query_pos, query_doc, offset + jnp.arange(block_rows, dtype=jnp.int32), bounds
        )
        scores = block_scores(query_heads, key_block, allowed, score_scale)
        new_max = jnp.maximum(run_max, jnp.max(scores, axis=2))
        exp_weights = jnp.where(allowed, jnp.exp(scores - new_max[:, :, None]), 0.0)
        rescale = jnp.exp(run_max - new_max)
        run_total = run_total * rescale + jnp.sum(exp_weights, axis=2)
        weighted = weighted * rescale[:, :, None] + jnp.einsum(
            "bht,td->bhd",
            exp_weights.astype(jnp.bfloat16),
            value_block,
            preferred_element_type=jnp.float32,
        )
        return ((new_max, run_total, weighted), None)

    run_state, _ = lax.scan(forward_update, run_state, stacked)
    return run_state


def backward_piece(key_piece, value_piece, context):
    query_heads, grad_heads, query_pos, query_doc, bounds, score_scale, log_total, out_dot = context
    stacked, block_rows = key_blocks(key_piece, value_piece)

    def backward_update(query_sum, block_item):
        key_block, value_block, offset = block_item
        allowed = visible(
            query_pos, query_doc, offset + jnp.arange(block_rows, dtype=jnp.int32), bounds
        )
        scores = block_scores(query_heads, key_block, allowed, score_scale)
        weights = jnp.where(allowed, jnp.exp(scores - log_total[:, :, None]), 0.0)
        grad_dots = jnp.einsum(
            "bhd,td->bht", grad_heads, value_block, preferred_element_type=jnp.float32
        )
        score_grads = (weights * (grad_dots - out_dot[:, :, None])).astype(jnp.bfloat16)
        query_sum = query_sum + jnp.einsum(
            "bht,td->bhd", score_grads, key_block, preferred_element_type=jnp.float32
        )
        key_term = (
            jnp.einsum("bht,bhd->td", score_grads, query_heads, preferred_element_type=jnp.float32)
            * score_scale
        )
        value_term = jnp.einsum(
            "bht,bhd->td",
            weights.astype(jnp.bfloat16),
            grad_heads,
            preferred_element_type=jnp.float32,
        )
        return (query_sum, (key_term, value_term))

    zero_query = jnp.zeros(query_heads.shape, jnp.float32)
    query_add, (key_terms, value_terms) = lax.scan(backward_update, zero_query, stacked)
    piece_rows = key_piece.shape[0]
    return (query_add, key_terms.reshape(piece_rows, -1), value_terms.reshape(piece_rows, -1))


def per_device(queries, keys, values, grad_out, lengths, send_order):
    shard_count = lax.axis_size("seq")
    my_index = lax.axis_index("seq")
    tok_rows, head_dim = keys.shape
    group_rows = tok_rows // shard_count
    head_count = queries.shape[1] // head_dim
    score_scale = 1.0 / math.sqrt(head_dim)
    bounds = jnp.cumsum(lengths)
    own_order = lax.dynamic_index_in_dim(send_order, my_index, 0, keepdims=False)
    outgoing = jnp.take(queries, own_order, axis=0)
    picked = lax.all_to_all(outgoing, "seq", split_axis=0, concat_axis=0, tiled=True)
    columns = lax.dynamic_slice_in_dim(send_order, my_index * group_rows, group_rows, 1)
    query_pos = (jnp.arange(shard_count, dtype=jnp.int32)[:, None] * tok_rows + columns).reshape(
        tok_rows
    )
    query_doc = doc_index(query_pos, bounds)
    query_heads = picked.reshape(tok_rows, head_count, head_dim)
    grad_heads = grad_out.reshape(tok_rows, head_count, head_dim)
    context = (query_heads, query_pos, query_doc, bounds, score_scale)
    start_state = (
        jnp.full((tok_rows, head_count), masked_value, jnp.float32),
        jnp.zeros((tok_rows, head_count), jnp.float32),
        jnp.zeros((tok_rows, head_count, head_dim), jnp.float32),
    )
    piece_pair = (
        lax.all_gather(keys, "seq", axis=0, tiled=True),
        lax.all_gather(values, "seq", axis=0, tiled=True),
    )
    run_max, run_total, weighted = forward_piece(start_state, piece_pair[0], piece_pair[1], context)
    attended = weighted / run_total[:, :, None]
    attended_low = attended.astype(jnp.bfloat16)
    log_total = run_max + jnp.log(run_total)
    out_dot = jnp.sum(grad_heads.astype(jnp.float32) * attended_low.astype(jnp.float32), axis=2)
    grad_context = (
        query_heads,
        grad_heads,
        query_pos,
        query_doc,
        bounds,
        score_scale,
        log_total,
        out_dot,
    )
    piece_pair = (
        lax.all_gather(keys, "seq", axis=0, tiled=True),
        lax.all_gather(values, "seq", axis=0, tiled=True),
    )
    query_add, key_part, value_part = backward_piece(piece_pair[0], piece_pair[1], grad_context)
    key_all = key_part
    value_all = value_part
    query_sum, key_all, value_all = (query_add, key_all, value_all)
    key_grad, value_grad = (
        lax.psum_scatter(key_all, "seq", scatter_dimension=0, tiled=True),
        lax.psum_scatter(value_all, "seq", scatter_dimension=0, tiled=True),
    )
    grad_queries = (query_sum * score_scale).reshape(tok_rows, head_count * head_dim)
    return (attended.reshape(tok_rows, head_count * head_dim), grad_queries, key_grad, value_grad)


def solution(mesh):
    placed = (P("seq", "head"), P("seq", "head"), P("seq", "head"), P("seq", "head"), P(), P())
    return jax.shard_map(
        per_device,
        mesh=mesh,
        in_specs=placed,
        out_specs=(P("seq", "head"), P("seq", "head"), P("seq", "head"), P("seq", "head")),
        check_vma=False,
    )
```

profile of v0, /device:TPU:0, one launch (start us, length us, event | category | flops | bytes accessed | tf_op | source)
XLA Modules:
  0.0 495.6 jit_solution(17738057707198617605)
XLA Ops:
  12.2 8.4 %all-to-all-start = ((bf16[32,8,512]{2,1,0:T(8,128)(2,1)}), bf16[32,8,512]{2,1,0:T(8,128)(2,1)S(1)}, u32[]{:S(2)}, u32[]{:S(2)}) async-start(bf16[32,8,512]{2,1,0:T(8,128)(2,1)} %bitcast_select_fusion.2), calls=%async_computation | async-start | bytes 524288 | tf_op jit(solution)/shard_map/all_to_all | solution.py:115
  21.8 8.0 %all-to-all-done = bf16[32,8,512]{2,1,0:T(8,128)(2,1)S(1)} async-done(((bf16[32,8,512]{2,1,0:T(8,128)(2,1)}), bf16[32,8,512]{2,1,0:T(8,128)(2,1)S(1)}, u32[]{:S(2)}, u32[]{:S(2)}) %all-to-all-start) | async-done | bytes 262176 | tf_op jit(solution)/shard_map/all_to_all | solution.py:115
  29.9 26.8 %all-gather.3.cloned.1.call-done = bf16[8192,128]{1,0:T(8,128)(2,1)} async-done(((bf16[256,128]{1,0:T(8,128)(2,1)}), bf16[8192,128]{1,0:T(8,128)(2,1)}) %all-gather.3.cloned.1.call-update) | async-done | bytes 2097168 | tf_op jit(solution)/shard_map/all_gather | solution.py:130
  56.7 45.3 %all-gather.5.cloned.1.call-done = bf16[8192,128]{1,0:T(8,128)(2,1)} async-done(((bf16[256,128]{1,0:T(8,128)(2,1)}), bf16[8192,128]{1,0:T(8,128)(2,1)}) %all-gather.5.cloned.1.call-update) | async-done | bytes 2097168 | tf_op jit(solution)/shard_map/all_gather | solution.py:131
  102.0 85.3 %while.32 = (s32[]{:T(128)}, f32[256,4]{0,1:T(4,128)S(1)}, f32[256,4]{0,1:T(4,128)S(1)}, f32[256,4,128]{2,0,1:T(8,128)S(1)}, s32[256]{0:T(256)S(1)}, /*index=5*/...) while((s32[]{:T(128)}, f32[256,4]{0,1:T(4,128)S(1)}, ...), condition=%wide.wide.region_6.7_spmd.clone, body=%wide.wide.region_2.6_spmd.clone.sunk | while | flops 276067328 | bytes 8466673 | solution.py:65
  105.5 1.8 convolution_add_fusion.6
  110.8 1.8 convolution_add_fusion.6
  116.2 1.8 convolution_add_fusion.6
  121.5 1.8 convolution_add_fusion.6
  126.8 1.8 convolution_add_fusion.6
  132.1 1.8 convolution_add_fusion.6
  137.5 1.8 convolution_add_fusion.6
  142.8 1.8 convolution_add_fusion.6
  148.1 1.8 convolution_add_fusion.6
  153.5 1.8 convolution_add_fusion.6
  158.8 1.8 convolution_add_fusion.6
  164.1 1.8 convolution_add_fusion.6
  169.5 1.8 convolution_add_fusion.6
  174.8 1.8 convolution_add_fusion.6
  180.1 1.8 convolution_add_fusion.6
  185.5 1.8 convolution_add_fusion.6
  187.6 133.8 %while.33 = (s32[]{:T(128)}, f32[256,4,128]{2,0,1:T(8,128)S(1)}, f32[16,512,128]{2,1,0:T(8,128)}, f32[16,512,128]{2,1,0:T(8,128)}, s32[256]{0:T(256)S(1)}, /*ind...) while((s32[]{:T(128)}, f32[256,4,128]{2,0,1:T(8,128)S(1)}, ...), condition=%wide.wide.region_10.11_spmd.clone, body=%wide.wide.region_8.10_spmd.clone.sunk | while | flops 676028416 | bytes 12734739 | solution.py:100
  189.1 1.6 fusion.101
  192.1 1.6 convolution_add_fusion.7
  197.5 1.6 fusion.101
  200.4 1.6 convolution_add_fusion.7
  205.8 1.6 fusion.101
  214.2 1.6 fusion.101
  222.6 1.6 fusion.101
  230.9 1.6 fusion.101
  239.3 1.6 fusion.101
  247.7 1.6 fusion.101
  250.6 1.6 convolution_add_fusion.7
  256.0 1.6 fusion.101
  259.0 1.6 convolution_add_fusion.7
  264.4 1.6 fusion.101
  272.8 1.6 fusion.101
  275.7 1.6 convolution_add_fusion.7
  281.1 1.6 fusion.101
  289.5 1.6 fusion.101
  292.5 1.6 convolution_add_fusion.7
  297.9 1.6 fusion.101
  300.8 1.6 convolution_add_fusion.7
  306.2 1.6 fusion.101
  309.2 1.6 convolution_add_fusion.7
  314.6 1.6 fusion.101
  323.9 79.4 %reduce-scatter.5.cloned.1.call-done = f32[256,128]{1,0:T(8,128)} async-done(((f32[8192,128]{1,0:T(8,128)}), f32[256,128]{1,0:T(8,128)}) %reduce-scatter.5.cloned.1.call-update) | async-done | bytes 131088 | tf_op jit(solution)/shard_map/reduce_scatter | solution.py:158
  403.3 85.8 %reduce-scatter.3.cloned.1.call-done = f32[256,128]{1,0:T(8,128)} async-done(((f32[8192,128]{1,0:T(8,128)}), f32[256,128]{1,0:T(8,128)}) %reduce-scatter.3.cloned.1.call-update) | async-done | bytes 131088 | tf_op jit(solution)/shard_map/reduce_scatter | solution.py:157
  (314 shorter events, 159.5 us)
Async XLA Ops:
  7.2 3.1 copy-start
  7.2 13.5 %copy-start.3 = (s32[32,256]{1,0:T(8,128)S(1)}, s32[32,256]{1,0:T(8,128)}, u32[]{:S(2)}) copy-start(s32[32,256]{1,0:T(8,128)} %param.15) | copy-start | bytes 98308
  7.2 13.9 %copy-start.4 = (s32[16]{0:T(128)S(1)}, s32[16]{0:T(128)}, u32[]{:S(2)}) copy-start(s32[16]{0:T(128)} %param.14) | copy-start | bytes 196
  7.2 14.2 %copy-start.1 = (bf16[256,512]{1,0:T(8,128)(2,1)S(1)}, bf16[256,512]{1,0:T(8,128)(2,1)}, u32[]{:S(2)}) copy-start(bf16[256,512]{1,0:T(8,128)(2,1)} %param.13) | copy-start | bytes 786436
  7.2 49.5 %all-gather.3.cloned.1.call-start = ((), (), s32[]{:S(2)}) async-start(), calls=%async_computation.3 | async-start | bytes 2162688 | tf_op jit(solution)/shard_map/all_gather | solution.py:130
  7.9 94.0 %all-gather.5.cloned.1.call-start = ((), (), s32[]{:S(2)}) async-start(), calls=%async_computation.4 | async-start | bytes 2162688 | tf_op jit(solution)/shard_map/all_gather | solution.py:131
  12.2 17.5 %all-to-all-start = ((bf16[32,8,512]{2,1,0:T(8,128)(2,1)}), bf16[32,8,512]{2,1,0:T(8,128)(2,1)S(1)}, u32[]{:S(2)}, u32[]{:S(2)}) async-start(bf16[32,8,512]{2,1,0:T(8,128)(2,1)} %bitcast_select_fusion.2), calls=%async_computation | async-start | bytes 524288 | tf_op jit(solution)/shard_map/all_to_all | solution.py:115
  20.7 382.6 %reduce-scatter.5.cloned.1.call-start = ((), (), s32[]{:S(2)}) async-start(), calls=%async_computation.6 | async-start | bytes 4325376 | tf_op jit(solution)/shard_map/reduce_scatter | solution.py:158
  20.8 81.2 %copy-start.2 = (s32[32,8]{1,0:T(8,128)}, s32[32,8]{1,0:T(8,128)S(1)}, u32[]{:S(2)}) copy-start(s32[32,8]{1,0:T(8,128)S(1)} %dynamic-slice_add_fusion) | copy-start | bytes 3076
  321.4 167.7 %reduce-scatter.3.cloned.1.call-start = ((), (), s32[]{:S(2)}) async-start(), calls=%async_computation.5 | async-start | bytes 4325376 | tf_op jit(solution)/shard_map/reduce_scatter | solution.py:157
Sparse Core Ops, SparseCore 0:
  10.3 46.3 all-gather.2
  59.0 42.9 all-gather.4
  321.5 81.6 reduce-scatter.4
  407.3 81.6 reduce-scatter.2
where the time goes:
time: 498 us; the launch traced here: 496 us
  waiting for transfers between devices  247 us (50%)
  matrix products  160 us (32%)
  other arithmetic  41.9 us (8%)
  local copies, waits for them, and re-layouts  22.7 us (5%)
  between operations  14 us (3%)
  starting transfers between devices  8.6 us (2%)
    reduce_scatter x1, waiting for transfers between devices, per_device(): lax.psum_scatter(key_all, 'seq', scatter_dimension=0, tiled=True)  85.8 us
    reduce_scatter x1, waiting for transfers between devices, per_device(): lax.psum_scatter(value_all, 'seq', scatter_dimension=0, tiled=True)  79.4 us
    dot_general x32, matrix products, block_scores(): jnp.einsum('bhd,td->bht', query_heads, key_block, preferred_element_type=...  47.9 us
    all_gather x1, waiting for transfers between devices, per_device(): lax.all_gather(values, 'seq', axis=0, tiled=True)  45.3 us
    dot_general x16, matrix products, forward_update(): jnp.einsum('bht,td->bhd', exp_weights.astype(jnp.bfloat16), value_block,...  28.7 us
    all_gather x1, waiting for transfers between devices, per_device(): lax.all_gather(keys, 'seq', axis=0, tiled=True)  26.8 us
    dot_general x16, matrix products, backward_update(): jnp.einsum('bht,td->bhd', score_grads, key_block, preferred_element_type=...  24.8 us
    dot_general x16, matrix products, backward_update(): jnp.einsum('bhd,td->bht', grad_heads, value_block, preferred_element_type...  21.5 us
  transfers between devices with their start and end apart: 5, of which 5 were waited for; matrix products, arithmetic and copies ran while one was open for 1% of the time, Pallas kernels for 0%

commit v1 on v0

--- a/solution.py
+++ b/solution.py
@@ -5,6 +5,15 @@
 from jax.sharding import PartitionSpec as P
 
 masked_value = -1e30
+
+
+def draft_axis_part(x_in, on_dim):
+    newest = lax.axis_size("seq")
+    current_arr = jnp.concatenate(newest * [x_in], on_dim)
+    current_block = lax.all_to_all(
+        current_arr, axis_name="seq", split_axis=on_dim, concat_axis=on_dim, tiled=True
+    )
+    return current_block
 
 
 def doc_index(positions, bounds):
@@ -126,10 +135,7 @@
         jnp.zeros((tok_rows, head_count), jnp.float32),
         jnp.zeros((tok_rows, head_count, head_dim), jnp.float32),
     )
-    piece_pair = (
-        lax.all_gather(keys, "seq", axis=0, tiled=True),
-        lax.all_gather(values, "seq", axis=0, tiled=True),
-    )
+    piece_pair = (lax.all_gather(keys, "seq", axis=0, tiled=True), draft_axis_part(values, 0))
     run_max, run_total, weighted = forward_piece(start_state, piece_pair[0], piece_pair[1], context)
     attended = weighted / run_total[:, :, None]
     attended_low = attended.astype(jnp.bfloat16)

time: 498 us -> 472 us (0.948)
  waiting for transfers between devices: 247 us -> 194 us
  local copies, waits for them, and re-layouts: 22.7 us -> 42.6 us
  starting transfers between devices: 8.6 us -> 16.3 us
    all_gather x1, waiting for transfers between devices: 45.3 us -> 0.02 us  [per_device(): lax.all_gather(values, 'seq', axis=0, tiled=True)]
    all_to_all x0 -> x1, waiting for transfers between devices: none -> 28 us  [draft_axis_part(): lax.all_to_all(current_arr, axis_name='seq', split_axis=on_dim, concat_ax...]
    all_gather x1, waiting for transfers between devices: 26.8 us -> 0.01 us  [per_device(): lax.all_gather(keys, 'seq', axis=0, tiled=True)]
    unnamed x14 -> x47, local copies, waits for them, and re-layouts: 1.36 us -> 20.7 us
    all_to_all x1, waiting for transfers between devices: 7.96 us -> 0.01 us  [per_device(): lax.all_to_all(outgoing, 'seq', split_axis=0, concat_axis=0, tiled=True)]
    all_to_all x0 -> x1, starting transfers between devices: none -> 7.65 us  [draft_axis_part(): lax.all_to_all(current_arr, axis_name='seq', split_axis=on_dim, concat_ax...]
  transfers between devices with their start and end apart: 5 -> 6, of which waited for: 5 -> 3; matrix products, arithmetic and copies ran while one was open for 1% -> 24% of each run, Pallas kernels for 0% -> 0%
where the time goes in v1:
time: 472 us; the launch traced here: 470 us
  waiting for transfers between devices  194 us (41%)
  matrix products  160 us (34%)
  local copies, waits for them, and re-layouts  42.6 us (9%)
  other arithmetic  41.9 us (9%)
  starting transfers between devices  16.3 us (3%)
  between operations  14 us (3%)
    reduce_scatter x1, waiting for transfers between devices, per_device(): lax.psum_scatter(key_all, 'seq', scatter_dimension=0, tiled=True)  85.9 us
    reduce_scatter x1, waiting for transfers between devices, per_device(): lax.psum_scatter(value_all, 'seq', scatter_dimension=0, tiled=True)  77.9 us
    dot_general x32, matrix products, block_scores(): jnp.einsum('bhd,td->bht', query_heads, key_block, preferred_element_type=...  47.9 us
    dot_general x16, matrix products, forward_update(): jnp.einsum('bht,td->bhd', exp_weights.astype(jnp.bfloat16), value_block,...  28.7 us
    all_to_all x1, waiting for transfers between devices, draft_axis_part(): lax.all_to_all(current_arr, axis_name='seq', split_axis=on_dim, concat_ax...  28 us
    dot_general x16, matrix products, backward_update(): jnp.einsum('bht,td->bhd', score_grads, key_block, preferred_element_type=...  24.9 us
    dot_general x16, matrix products, backward_update(): jnp.einsum('bhd,td->bht', grad_heads, value_block, preferred_element_type...  21.5 us
    unnamed x47, local copies, waits for them, and re-layouts  20.7 us
  transfers between devices with their start and end apart: 6, of which 3 were waited for; matrix products, arithmetic and copies ran while one was open for 24% of the time, Pallas kernels for 0%

profile of v1, /device:TPU:0, one launch (start us, length us, event | category | flops | bytes accessed | tf_op | source)
XLA Modules:
  0.0 469.8 jit_solution(7992012147603851528)
XLA Ops:
  11.4 8.4 %all-to-all-start = ((bf16[32,8,512]{2,1,0:T(8,128)(2,1)}), bf16[32,8,512]{2,1,0:T(8,128)(2,1)S(1)}, u32[]{:S(2)}, u32[]{:S(2)}) async-start(bf16[32,8,512]{2,1,0:T(8,128)(2,1)} %bitcast_select_fusion.2), calls=%async_computation | async-start | bytes 524288 | tf_op jit(solution)/shard_map/all_to_all | solution.py:124
  39.8 7.7 %all-to-all-start.1 = ((bf16[32,256,128]{2,1,0:T(8,128)(2,1)}), bf16[32,256,128]{2,1,0:T(8,128)(2,1)}, u32[]{:S(2)}, u32[]{:S(2)}) async-start(bf16[32,256,128]{2,1,0:T(8,128)(2,1)} %bitcast.5), calls=%async_computation.1 | async-start | bytes 4194304 | tf_op jit(solution)/shard_map/all_to_all | solution.py:13
  49.5 28.0 %all-to-all-done.1 = bf16[32,256,128]{2,1,0:T(8,128)(2,1)} async-done(((bf16[32,256,128]{2,1,0:T(8,128)(2,1)}), bf16[32,256,128]{2,1,0:T(8,128)(2,1)}, u32[]{:S(2)}, u32[]{:S(2)}) %all-to-all-start.1) | async-done | bytes 2097184 | tf_op jit(solution)/shard_map/all_to_all | solution.py:13
  77.6 85.3 %while.32 = (s32[]{:T(128)}, f32[256,4]{0,1:T(4,128)S(1)}, f32[256,4]{0,1:T(4,128)S(1)}, f32[256,4,128]{2,0,1:T(8,128)S(1)}, s32[256]{0:T(256)S(1)}, /*index=5*/...) while((s32[]{:T(128)}, f32[256,4]{0,1:T(4,128)S(1)}, ...), condition=%wide.wide.region_6.7_spmd.clone, body=%wide.wide.region_2.6_spmd.clone.sunk | while | flops 276067328 | bytes 8466673 | solution.py:74
  81.1 1.8 convolution_add_fusion.6
  86.4 1.8 convolution_add_fusion.6
  91.7 1.8 convolution_add_fusion.6
  97.1 1.8 convolution_add_fusion.6
  102.4 1.8 convolution_add_fusion.6
  107.7 1.8 convolution_add_fusion.6
  113.1 1.8 convolution_add_fusion.6
  118.4 1.8 convolution_add_fusion.6
  123.7 1.8 convolution_add_fusion.6
  129.0 1.8 convolution_add_fusion.6
  134.4 1.8 convolution_add_fusion.6
  139.7 1.8 convolution_add_fusion.6
  145.0 1.8 convolution_add_fusion.6
  150.4 1.8 convolution_add_fusion.6
  155.7 1.8 convolution_add_fusion.6
  161.0 1.8 convolution_add_fusion.6
  163.2 133.8 %while.33 = (s32[]{:T(128)}, f32[256,4,128]{2,0,1:T(8,128)S(1)}, f32[16,512,128]{2,1,0:T(8,128)}, f32[16,512,128]{2,1,0:T(8,128)}, s32[256]{0:T(256)S(1)}, /*ind...) while((s32[]{:T(128)}, f32[256,4,128]{2,0,1:T(8,128)S(1)}, ...), condition=%wide.wide.region_10.11_spmd.clone, body=%wide.wide.region_8.10_spmd.clone.sunk | while | flops 676028416 | bytes 12734739 | solution.py:109
  164.8 1.6 fusion.101
  173.1 1.6 fusion.101
  181.4 1.6 fusion.101
  184.4 1.6 convolution_add_fusion.7
  189.8 1.6 fusion.101
  192.7 1.6 convolution_add_fusion.7
  198.2 1.6 fusion.101
  201.1 1.6 convolution_add_fusion.7
  206.5 1.6 fusion.101
  209.5 1.6 convolution_add_fusion.7
  214.9 1.6 fusion.101
  223.3 1.6 fusion.101
  231.6 1.6 fusion.101
  240.0 1.6 fusion.101
  243.0 1.6 convolution_add_fusion.7
  248.4 1.6 fusion.101
  251.3 1.6 convolution_add_fusion.7
  256.7 1.6 fusion.101
  259.7 1.6 convolution_add_fusion.7
  265.1 1.6 fusion.101
  268.1 1.6 convolution_add_fusion.7
  273.5 1.6 fusion.101
  281.8 1.6 fusion.101
  290.2 1.6 fusion.101
  293.1 1.6 convolution_add_fusion.7
  299.5 77.9 %reduce-scatter.5.cloned.1.call-done = f32[256,128]{1,0:T(8,128)} async-done(((f32[8192,128]{1,0:T(8,128)}), f32[256,128]{1,0:T(8,128)}) %reduce-scatter.5.cloned.1.call-update) | async-done | bytes 131088 | tf_op jit(solution)/shard_map/reduce_scatter | solution.py:164
  377.3 85.9 %reduce-scatter.3.cloned.1.call-done = f32[256,128]{1,0:T(8,128)} async-done(((f32[8192,128]{1,0:T(8,128)}), f32[256,128]{1,0:T(8,128)}) %reduce-scatter.3.cloned.1.call-update) | async-done | bytes 131088 | tf_op jit(solution)/shard_map/reduce_scatter | solution.py:163
  (350 shorter events, 177.9 us)
Async XLA Ops:
  7.2 2.3 copy-start
  7.2 12.7 %copy-start.1 = (bf16[256,128]{1,0:T(8,128)(2,1)S(1)}, bf16[256,128]{1,0:T(8,128)(2,1)}, u32[]{:S(2)}) copy-start(bf16[256,128]{1,0:T(8,128)(2,1)} %param.12) | copy-start | bytes 196612
  7.2 70.4 %all-gather.3.cloned.1.call-start = ((), (), s32[]{:S(2)}) async-start(), calls=%async_computation.4 | async-start | bytes 2162688 | tf_op jit(solution)/shard_map/all_gather | solution.py:138
  11.4 28.4 %all-to-all-start = ((bf16[32,8,512]{2,1,0:T(8,128)(2,1)}), bf16[32,8,512]{2,1,0:T(8,128)(2,1)S(1)}, u32[]{:S(2)}, u32[]{:S(2)}) async-start(bf16[32,8,512]{2,1,0:T(8,128)(2,1)} %bitcast_select_fusion.2), calls=%async_computation | async-start | bytes 524288 | tf_op jit(solution)/shard_map/all_to_all | solution.py:124
  39.8 8.5 %copy-start.4 = (s32[32,256]{1,0:T(8,128)S(1)}, s32[32,256]{1,0:T(8,128)}, u32[]{:S(2)}) copy-start(s32[32,256]{1,0:T(8,128)} %param.15) | copy-start | bytes 98308
  39.8 8.9 %copy-start.5 = (s32[16]{0:T(128)S(1)}, s32[16]{0:T(128)}, u32[]{:S(2)}) copy-start(s32[16]{0:T(128)} %param.14) | copy-start | bytes 196
  39.8 9.2 %copy-start.2 = (bf16[256,512]{1,0:T(8,128)(2,1)S(1)}, bf16[256,512]{1,0:T(8,128)(2,1)}, u32[]{:S(2)}) copy-start(bf16[256,512]{1,0:T(8,128)(2,1)} %param.13) | copy-start | bytes 786436
  39.8 37.7 %all-to-all-start.1 = ((bf16[32,256,128]{2,1,0:T(8,128)(2,1)}), bf16[32,256,128]{2,1,0:T(8,128)(2,1)}, u32[]{:S(2)}, u32[]{:S(2)}) async-start(bf16[32,256,128]{2,1,0:T(8,128)(2,1)} %bitcast.5), calls=%async_computation.1 | async-start | bytes 4194304 | tf_op jit(solution)/shard_map/all_to_all | solution.py:13
  47.5 115.7 %all-gather.5.cloned.1.call-start = ((), (), s32[]{:S(2)}) async-start(), calls=%async_computation.5 | async-start | bytes 2162688 | tf_op jit(solution)/shard_map/all_gather | solution.py:156
  48.3 329.1 %reduce-scatter.5.cloned.1.call-start = ((), (), s32[]{:S(2)}) async-start(), calls=%async_computation.7 | async-start | bytes 4325376 | tf_op jit(solution)/shard_map/reduce_scatter | solution.py:164
  48.4 29.2 %copy-start.3 = (s32[32,8]{1,0:T(8,128)}, s32[32,8]{1,0:T(8,128)S(1)}, u32[]{:S(2)}) copy-start(s32[32,8]{1,0:T(8,128)S(1)} %dynamic-slice_add_fusion) | copy-start | bytes 3076
  297.0 166.2 %reduce-scatter.3.cloned.1.call-start = ((), (), s32[]{:S(2)}) async-start(), calls=%async_computation.6 | async-start | bytes 4325376 | tf_op jit(solution)/shard_map/reduce_scatter | solution.py:163
Sparse Core Ops, SparseCore 0:
  10.3 53.0 all-gather.2
  65.6 53.5 all-gather.4
  297.1 80.1 reduce-scatter.4
  381.4 81.7 reduce-scatter.2
